TPU v7x, 512 devices: a whole 4x4x16 slice. The times are simulated.
512 devices in a mesh: req: 128 (over z, x, core), tp: 4 (over y).
Axes of the slice: x: 4, y: 4, z: 16, core: 2. Of those that a mesh axis runs over, the one named last changes fastest.
Arguments:
- queries: bfloat16 [16384, 3584], P('req', 'tp'), may hold values from -13 to 13
- tree_kv: bfloat16 [16384, 4, 256], P('req', 'tp'), may hold values from -5 to 5
- page_pool: bfloat16 [1536, 4, 128, 256], P('req', 'tp'), may hold values from -5 to 5
- page_table: int32 [256, 8], P('req'), may hold values from 0 to 11, as said below
- cache_len: int32 [256], P('req'), may hold values from 1 to 1024
- parents: int32 [256, 64], P('req'), may hold values from -1 to 62, as said below
- accepted: int32 [256], P('req'), may hold values from 0 to 63
- o_weight: bfloat16 [3584, 1792], P('tp'), may hold values from -0.5 to 0.5
Outputs:
- projected: bfloat16 [16384, 1792], P(('req', 'tp'))
- kept_rows: bfloat16 [16384, 4, 256], P('req', 'tp')
Inputs may be any that keep to these rules, and one draw needn't show every extreme that they name: Logical page k of request r is in slot page_table[r, k] of its own device's pool for k < 2, among that pool's first 4 slots, and for k >= 2 in that slot of the next req device's pool (the first device after the last), among its last 8 slots; distinct pages are in distinct slots; entries at k >= ceil(cache_len[r] / 128) are 0. parents[r, 0] = -1 and 0 <= parents[r, j] < j for j >= 1.
All inputs are finite; a program needn't handle non-finite values.
Results may differ from a plain program's by a relative error of at most 0.007.
Values may be sent and summed in bfloat16 or wider, within the bound.
No kernel may reach another device: no remote copies, remote signals or barrier semaphores. Data moves between devices by JAX's collectives and lax.ppermute only.
A program may use at most 64 MiB of HBM per device.

v0:
```python
import functools
import math

import jax
import jax.numpy as jnp
from jax import lax
from jax.experimental import pallas as pl
from jax.experimental.pallas import tpu as pltpu
from jax.sharding import PartitionSpec as P

HEAD_SIZE = 128
LOCAL = 2

very_negative = -1e30


def nt_dot(a, b):
    return lax.dot_general(a, b, (((1,), (1,)), ((), ())), preferred_element_type=jnp.float32)


def stacked_queries(q_ref, rows, heads):
    q = q_ref[rows, :]
    return jnp.concatenate(
        [q[:, g * HEAD_SIZE : (g + 1) * HEAD_SIZE] for g in range(heads)], axis=0
    )


def page_blocks(q_all, pages, first_page, length):
    page_len = pages[0].shape[0]
    keys = jnp.concatenate([page[:, :HEAD_SIZE] for page in pages], axis=0)
    lane = lax.broadcasted_iota(jnp.int32, (1, keys.shape[0]), 1)
    visible = (first_page * page_len + lane) < length
    scores = nt_dot(q_all, keys) * (1.0 / math.sqrt(HEAD_SIZE))
    scores = jnp.where(visible, scores, very_negative)
    blocks = []
    for k, page in enumerate(pages):
        cols = slice(k * page_len, (k + 1) * page_len)
        s = scores[:, cols]
        m = jnp.max(s, axis=1, keepdims=True)
        w = jnp.exp(s - m).astype(jnp.bfloat16)
        l = jnp.sum(w.astype(jnp.float32), axis=1, keepdims=True)
        a = jnp.dot(w, page[:, HEAD_SIZE:], preferred_element_type=jnp.float32)
        blocks.append((m, l, a))
    return blocks


def merge(blocks):
    top = blocks[0][0]
    for m, _, _ in blocks[1:]:
        top = jnp.maximum(top, m)
    total = None
    accum = None
    for m, l, a in blocks:
        f = jnp.exp(m - top)
        total = f * l if total is None else total + f * l
        accum = f * a if accum is None else accum + f * a
    return top, total, accum


def local_kernel(
    table_ref, len_ref, leaf_ref, parents_ref, q_ref, tree_ref, pool_ref,
    kept_ref, ml_ref, a_ref, qs_ref,
):
    n_req, tree_len = parents_ref.shape
    nodes = n_req * tree_len
    heads = q_ref.shape[1] // HEAD_SIZE
    stacked = heads * tree_len
    scale = 1.0 / math.sqrt(HEAD_SIZE)
    sub = lax.broadcasted_iota(jnp.int32, (nodes, nodes), 0)
    lane = lax.broadcasted_iota(jnp.int32, (nodes, nodes), 1)
    eye = (sub == lane).astype(jnp.float32)
    squarings = (tree_len - 1).bit_length()

    parents = parents_ref[...].astype(jnp.float32)
    first = lax.broadcasted_iota(jnp.int32, parents.shape, 0).astype(jnp.float32) * tree_len
    parents = jnp.where(parents >= 0.0, parents + first, -1.0).astype(jnp.bfloat16)
    node = lax.broadcasted_iota(jnp.int32, (tree_len, nodes), 0)
    column = lax.broadcasted_iota(jnp.int32, (tree_len, nodes), 1)
    parent_row = None
    for r in range(n_req):
        place = (column == node + r * tree_len).astype(jnp.bfloat16)
        lhs = jnp.broadcast_to(parents[r : r + 1], (16, tree_len))
        placed = jnp.dot(lhs, place, preferred_element_type=jnp.float32)[0:1]
        parent_row = placed if parent_row is None else parent_row + placed

    rt = eye + (sub.astype(jnp.float32) == parent_row).astype(jnp.float32)
    for _ in range(squarings):
        rb = rt.astype(jnp.bfloat16)
        rt = jnp.minimum(jnp.dot(rb, rb, preferred_element_type=jnp.float32), 1.0)
    reach = nt_dot(eye.astype(jnp.bfloat16), rt.astype(jnp.bfloat16))

    depth = jnp.sum(rt, axis=0, keepdims=True) - 1.0
    slot = lax.broadcasted_iota(jnp.int32, (tree_len, nodes), 0).astype(jnp.float32)
    selectors = []
    for r in range(n_req):
        leaf = r * tree_len + leaf_ref[r]
        kept_mask = jnp.sum(jnp.where(sub == leaf, reach, 0.0), axis=0, keepdims=True)
        selectors.append(jnp.where((slot == depth) & (kept_mask > 0.5), 1.0, 0.0))
    selector = jnp.concatenate(selectors, axis=0).astype(jnp.bfloat16)
    tree_rows = tree_ref[...]
    kept_ref[...] = jnp.dot(selector, tree_rows, preferred_element_type=jnp.float32).astype(
        kept_ref.dtype
    )

    q_all = [stacked_queries(q_ref, pl.ds(r * tree_len, tree_len), heads) for r in range(n_req)]
    for r in range(n_req):
        qs_ref[r] = q_all[r]
    tree_mask = (
        jnp.concatenate(
            [reach[r * tree_len : (r + 1) * tree_len] for r in range(n_req) for _ in range(heads)],
            axis=0,
        )
        > 0.5
    )
    s = nt_dot(jnp.concatenate(q_all, axis=0), tree_rows[:, :HEAD_SIZE]) * scale
    s = jnp.where(tree_mask, s, very_negative)
    m = jnp.max(s, axis=1, keepdims=True)
    w = jnp.exp(s - m).astype(jnp.bfloat16)
    l = jnp.sum(w.astype(jnp.float32), axis=1, keepdims=True)
    a = jnp.dot(w, tree_rows[:, HEAD_SIZE:], preferred_element_type=jnp.float32)

    state_lane = lax.broadcasted_iota(jnp.int32, (stacked, HEAD_SIZE), 1)
    for r in range(n_req):
        rows = slice(r * stacked, (r + 1) * stacked)
        pages = [pool_ref[table_ref[r, k]] for k in range(LOCAL)]
        blocks = [(m[rows], l[rows], a[rows])] + page_blocks(q_all[r], pages, 0, len_ref[r])
        top, total, accum = merge(blocks)
        ml_ref[r] = jnp.where(state_lane == 0, top, jnp.where(state_lane == 1, total, 0.0))
        a_ref[r] = accum


def spill_kernel(
    spill_base, table_ref, len_ref, ml_ref, a_ref, q_ref, spill_ref, weight_hbm,
    proj_ref, weight_vmem, att_sc, weight_sem,
):
    weight_copy = pltpu.make_async_copy(weight_hbm, weight_vmem, weight_sem)
    weight_copy.start()
    n_req, tree_len = table_ref.shape[0], att_sc.shape[0] // table_ref.shape[0]
    heads = att_sc.shape[1] // HEAD_SIZE
    max_pages = table_ref.shape[1]
    spill_slots = spill_ref.shape[0]
    for r in range(n_req):
        rows = pl.ds(r * tree_len, tree_len)
        q_all = q_ref[r]
        pages = [
            spill_ref[jnp.clip(table_ref[r, k] - spill_base, 0, spill_slots - 1)]
            for k in range(LOCAL, max_pages)
        ]
        ml = ml_ref[r]
        state = (ml[:, 0:1], ml[:, 1:2], a_ref[r])
        _, total, accum = merge([state] + page_blocks(q_all, pages, LOCAL, len_ref[r]))
        att = (accum / total).astype(att_sc.dtype)
        for g in range(heads):
            att_sc[rows, pl.ds(g * HEAD_SIZE, HEAD_SIZE)] = att[g * tree_len : (g + 1) * tree_len]

    weight_copy.wait()
    proj_ref[...] = jnp.dot(
        att_sc[...], weight_vmem[...], preferred_element_type=jnp.float32
    ).astype(proj_ref.dtype)


def step(queries, tree_kv, page_pool, page_table, cache_len, parents, accepted, o_weight):
    requests, tree_len = parents.shape
    heads = queries.shape[1] // HEAD_SIZE
    pool_slots = page_pool[:, 0]
    own_slots = requests * LOCAL
    ring = lax.axis_size("req")
    spill_source = pool_slots[own_slots:]
    spill = lax.ppermute(spill_source, "req", [((i + 1) % ring, i) for i in range(ring)])
    tree_rows = tree_kv[:, 0, :]
    smem = pl.BlockSpec(memory_space=pltpu.SMEM)
    vmem = pl.BlockSpec(memory_space=pltpu.VMEM)
    stacked = heads * tree_len
    local_call = pl.pallas_call(
        local_kernel,
        out_shape=(
            jax.ShapeDtypeStruct(tree_rows.shape, jnp.bfloat16),
            jax.ShapeDtypeStruct((requests, stacked, HEAD_SIZE), jnp.float32),
            jax.ShapeDtypeStruct((requests, stacked, HEAD_SIZE), jnp.float32),
            jax.ShapeDtypeStruct((requests, stacked, HEAD_SIZE), jnp.bfloat16),
        ),
        in_specs=[smem, smem, smem, vmem, vmem, vmem, vmem],
        out_specs=(vmem, vmem, vmem, vmem),
    )
    kept, packed, accum, stacked_q = local_call(
        page_table, cache_len, accepted, parents, queries, tree_rows, pool_slots
    )
    partial = pl.pallas_call(
        functools.partial(spill_kernel, own_slots),
        out_shape=jax.ShapeDtypeStruct((queries.shape[0], o_weight.shape[1]), jnp.bfloat16),
        in_specs=[smem, smem, vmem, vmem, vmem, vmem, pl.BlockSpec(memory_space=pl.ANY)],
        out_specs=vmem,
        scratch_shapes=[
            pltpu.VMEM(o_weight.shape, o_weight.dtype),
            pltpu.VMEM(queries.shape, jnp.bfloat16),
            pltpu.SemaphoreType.DMA(()),
        ],
    )(page_table, cache_len, packed, accum, stacked_q, spill, o_weight)

    parts = lax.axis_size("tp")
    gathered = lax.all_to_all(partial, "tp", 0, 0, tiled=True)
    blocks = gathered.reshape(parts, partial.shape[0] // parts, partial.shape[1])
    summed = blocks[0].astype(jnp.float32)
    for i in range(1, parts):
        summed = summed + blocks[i].astype(jnp.float32)
    projected = summed.astype(jnp.bfloat16)
    return (projected, kept.reshape(kept.shape[0], 1, kept.shape[1]))


def solution(mesh):
    in_specs = (
        P("req", "tp"),
        P("req", "tp", None),
        P("req", "tp", None, None),
        P("req", None),
        P("req"),
        P("req", None),
        P("req"),
        P("tp", None),
    )
    out_specs = (P(("req", "tp"), None), P("req", "tp", None))
    return jax.shard_map(step, mesh=mesh, in_specs=in_specs, out_specs=out_specs, check_vma=False)
```

profile of v0, /device:TPU:8, one launch (start us, length us, event | category | flops | bytes accessed | tf_op | source)
XLA Modules:
  0.0 40.4 jit_solution(16896002220845708165)
XLA Ops:
  0.6 1.1 %slice_bitcast_fusion = bf16[8,128,256]{2,1,0:T(8,128)(2,1)S(1)} fusion(bf16[12,1,128,256]{3,2,0,1:T(8,128)(2,1)} %bitcast.9), kind=kLoop, calls=%fused_computation | loop fusion | bytes 1048576 | tf_op jit(solution)/shard_map/slice | solution.py:168
  1.7 13.0 %collective-permute-start = (bf16[8,128,256]{2,1,0:T(8,128)(2,1)S(1)}, bf16[8,128,256]{2,1,0:T(8,128)(2,1)S(1)}, u32[]{:S(2)}, u32[]{:S(2)}) collective-permute-start(bf16[8,128,256]{2,1,0:T(8,128)(2,1)S(1)} %slice_bitcast_fusion), channel_id=1, source_target_pairs={{4,0},{8,4},{12,8},{16,12},{20,16},{24,20},{28,24},{32,28},{36,32}... | collective-permute-start | bytes 1572872 | tf_op jit(solution)/shard_map/ppermute | solution.py:169
  14.8 4.5 %shard_map.95 = (bf16[128,256]{1,0:T(8,128)(2,1)}, f32[2,448,128]{2,1,0:T(8,128)}, f32[2,448,128]{2,1,0:T(8,128)}, bf16[2,448,128]{2,1,0:T(8,128)(2,1)}) custom-call(s32[2,8]{1,0:T(2,128)} %table_ref.3, s32[2]{0:T(128)} %len_ref.3, s32[2]{0:T(128)} %leaf_ref.1, s32[2,64]{1,0:T(2,128)} %parents_ref.1, bf16[128,896]{1,0:T(8,128)(2,1)} %q_ref.1, ...), custom_call_target="tpu_custom_call" | custom-call | tf_op jit(solution)/shard_map/pallas_call | solution.py:185
  19.3 2.1 %collective-permute-done.spill_ref = bf16[8,128,256]{2,1,0:T(8,128)(2,1)S(1)} collective-permute-done((bf16[8,128,256]{2,1,0:T(8,128)(2,1)S(1)}, bf16[8,128,256]{2,1,0:T(8,128)(2,1)S(1)}, u32[]{:S(2)}, u32[]{:S(2)}) %collective-permute-start) | collective-permute-done | bytes 524320 | tf_op jit(solution)/shard_map/ppermute | solution.py:169
  21.4 0.0 copy-start
  21.4 0.8 %copy-done = bf16[8,128,256]{2,1,0:T(8,128)(2,1)} copy-done((bf16[8,128,256]{2,1,0:T(8,128)(2,1)}, bf16[8,128,256]{2,1,0:T(8,128)(2,1)S(1)}, u32[]{:S(2)}) %copy-start) | copy-done | bytes 524312
  22.2 6.2 %shard_map.96 = bf16[128,1792]{1,0:T(8,128)(2,1)} custom-call(s32[2,8]{1,0:T(2,128)} %table_ref.3, s32[2]{0:T(128)} %len_ref.3, f32[2,448,128]{2,1,0:T(8,128)} %get-tuple-element.6.ml_ref, f32[2,448,128]{2,1,0:T(8,128)} %get-tuple-element.7.a_ref, bf16[2,448,128]{2,1,0:T(8,128)(2,1)} %get-tuple-element.8.q_ref, bf16[8,128,256]{2,1,0:T(8,128)(2,1)} %copy-done, ...), custom_call_target="tpu_custom_call" | custom-call | tf_op jit(solution)/shard_map/pallas_call | solution.py:188
  28.5 11.2 %all_to_all.9 = bf16[4,32,1792]{2,1,0:T(8,128)(2,1)S(1)} all-to-all(bf16[4,32,1792]{2,1,0:T(8,128)(2,1)} %bitcast.11), channel_id=1, replica_groups=mesh['req'=128,'tp'=4] {'tp'}, dimensions={0} | all-to-all | bytes 917504 | tf_op jit(solution)/shard_map/all_to_all | solution.py:201
  39.7 0.7 %fusion = bf16[32,1792]{1,0:T(8,128)(2,1)} fusion(bf16[4,32,1792]{2,1,0:T(8,128)(2,1)S(1)} %all_to_all.9), kind=kLoop, calls=%fused_computation.2 | loop fusion | flops 458752 | bytes 573440 | tf_op jit(solution)/shard_map/add | solution.py:205
Async XLA Ops:
  1.7 19.7 %collective-permute-start = (bf16[8,128,256]{2,1,0:T(8,128)(2,1)S(1)}, bf16[8,128,256]{2,1,0:T(8,128)(2,1)S(1)}, u32[]{:S(2)}, u32[]{:S(2)}) collective-permute-start(bf16[8,128,256]{2,1,0:T(8,128)(2,1)S(1)} %slice_bitcast_fusion), channel_id=1, source_target_pairs={{4,0},{8,4},{12,8},{16,12},{20,16},{24,20},{28,24},{32,28},{36,32}... | collective-permute-start | bytes 1572872 | tf_op jit(solution)/shard_map/ppermute | solution.py:169
  21.4 0.8 %copy-start = (bf16[8,128,256]{2,1,0:T(8,128)(2,1)}, bf16[8,128,256]{2,1,0:T(8,128)(2,1)S(1)}, u32[]{:S(2)}) copy-start(bf16[8,128,256]{2,1,0:T(8,128)(2,1)S(1)} %collective-permute-done.spill_ref) | copy-start | bytes 1572868
where the time goes:
time: 40.6 us; the launch traced here: 40.4 us
  starting transfers between devices  13 us (32%)
  blocking collectives  11.2 us (28%)
  Pallas kernels  10.8 us (27%)
  waiting for transfers between devices  2.15 us (5%)
  local copies, waits for them, and re-layouts  1.87 us (5%)
  other arithmetic  0.7 us (2%)
  between operations  0.65 us (2%)
    ppermute x1, starting transfers between devices, step(): lax.ppermute(spill_source, 'req', [((i + 1) % ring, i) for i in range(rin...  13 us
    all_to_all x1, blocking collectives, step(): gathered = lax.all_to_all(partial, 'tp', 0, 0, tiled=True)  11.2 us
    pallas_call x1, Pallas kernels, step(): pl.pallas_call(functools.partial(spill_kernel, own_slots), out_shape=jax....  6.23 us
    pallas_call x1, Pallas kernels, step(): local_call(page_table, cache_len, accepted, parents, queries, tree_rows,...  4.53 us
    ppermute x1, waiting for transfers between devices, step(): lax.ppermute(spill_source, 'req', [((i + 1) % ring, i) for i in range(rin...  2.15 us
    slice x1, local copies, waits for them, and re-layouts, step(): spill_source = pool_slots[own_slots:]  1.08 us
  transfers between devices with their start and end apart: 1, of which 1 were waited for; matrix products, arithmetic and copies ran while one was open for 0% of the time, Pallas kernels for 11%

commit v1 on v0

--- a/solution.py
+++ b/solution.py
@@ -195,7 +195,10 @@
             pltpu.VMEM(queries.shape, jnp.bfloat16),
             pltpu.SemaphoreType.DMA(()),
         ],
-    )(page_table, cache_len, packed, accum, stacked_q, spill, o_weight)
+    )(
+        page_table, cache_len, packed, accum, stacked_q,
+        pltpu.with_memory_space_constraint(spill, pltpu.MemorySpace.VMEM), o_weight,
+    )
 
     parts = lax.axis_size("tp")
     gathered = lax.all_to_all(partial, "tp", 0, 0, tiled=True)

time: 40.6 us -> 39.7 us (0.978)
  local copies, waits for them, and re-layouts: 1.87 us -> 1.08 us
    unnamed x2 -> x0, local copies, waits for them, and re-layouts: 0.79 us -> none
where the time goes in v1:
time: 39.7 us; the launch traced here: 39.4 us
  starting transfers between devices  13 us (33%)
  blocking collectives  11.2 us (28%)
  Pallas kernels  10.5 us (26%)
  waiting for transfers between devices  2.17 us (5%)
  local copies, waits for them, and re-layouts  1.08 us (3%)
  other arithmetic  0.7 us (2%)
  between operations  0.65 us (2%)
    ppermute x1, starting transfers between devices, step(): lax.ppermute(spill_source, 'req', [((i + 1) % ring, i) for i in range(rin...  13 us
    all_to_all x1, blocking collectives, step(): gathered = lax.all_to_all(partial, 'tp', 0, 0, tiled=True)  11.2 us
    pallas_call x1, Pallas kernels, step(): pl.pallas_call(functools.partial(spill_kernel, own_slots), out_shape=jax....  6.04 us
    pallas_call x1, Pallas kernels, step(): local_call(page_table, cache_len, accepted, parents, queries, tree_rows,...  4.51 us
    ppermute x1, waiting for transfers between devices, step(): lax.ppermute(spill_source, 'req', [((i + 1) % ring, i) for i in range(rin...  2.17 us
    slice x1, local copies, waits for them, and re-layouts, step(): spill_source = pool_slots[own_slots:]  1.08 us
  transfers between devices with their start and end apart: 1, of which 1 were waited for; matrix products, arithmetic and copies ran while one was open for 0% of the time, Pallas kernels for 11%

profile of v1, /device:TPU:8, one launch (start us, length us, event | category | flops | bytes accessed | tf_op | source)
XLA Modules:
  0.0 39.4 jit_solution(14494397047853313046)
XLA Ops:
  0.6 1.1 %slice_bitcast_fusion = bf16[8,128,256]{2,1,0:T(8,128)(2,1)S(1)} fusion(bf16[12,1,128,256]{3,2,0,1:T(8,128)(2,1)} %bitcast.9), kind=kLoop, calls=%fused_computation | loop fusion | bytes 1048576 | tf_op jit(solution)/shard_map/slice | solution.py:168
  1.7 13.0 %collective-permute-start = (bf16[8,128,256]{2,1,0:T(8,128)(2,1)S(1)}, bf16[8,128,256]{2,1,0:T(8,128)(2,1)S(1)}, u32[]{:S(2)}, u32[]{:S(2)}) collective-permute-start(bf16[8,128,256]{2,1,0:T(8,128)(2,1)S(1)} %slice_bitcast_fusion), channel_id=1, source_target_pairs={{4,0},{8,4},{12,8},{16,12},{20,16},{24,20},{28,24},{32,28},{36,32}... | collective-permute-start | bytes 1572872 | tf_op jit(solution)/shard_map/ppermute | solution.py:169
  14.8 4.5 %shard_map.95 = (bf16[128,256]{1,0:T(8,128)(2,1)}, f32[2,448,128]{2,1,0:T(8,128)}, f32[2,448,128]{2,1,0:T(8,128)}, bf16[2,448,128]{2,1,0:T(8,128)(2,1)}) custom-call(s32[2,8]{1,0:T(2,128)} %table_ref.3, s32[2]{0:T(128)} %len_ref.3, s32[2]{0:T(128)} %leaf_ref.1, s32[2,64]{1,0:T(2,128)} %parents_ref.1, bf16[128,896]{1,0:T(8,128)(2,1)} %q_ref.1, ...), custom_call_target="tpu_custom_call" | custom-call | tf_op jit(solution)/shard_map/pallas_call | solution.py:185
  19.3 2.2 %collective-permute-done.spill_ref = bf16[8,128,256]{2,1,0:T(8,128)(2,1)S(1)} collective-permute-done((bf16[8,128,256]{2,1,0:T(8,128)(2,1)S(1)}, bf16[8,128,256]{2,1,0:T(8,128)(2,1)S(1)}, u32[]{:S(2)}, u32[]{:S(2)}) %collective-permute-start) | collective-permute-done | bytes 524320 | tf_op jit(solution)/shard_map/ppermute | solution.py:169
  21.4 6.0 %shard_map.96 = bf16[128,1792]{1,0:T(8,128)(2,1)} custom-call(s32[2,8]{1,0:T(2,128)} %table_ref.3, s32[2]{0:T(128)} %len_ref.3, f32[2,448,128]{2,1,0:T(8,128)} %get-tuple-element.6.ml_ref, f32[2,448,128]{2,1,0:T(8,128)} %get-tuple-element.7.a_ref, bf16[2,448,128]{2,1,0:T(8,128)(2,1)} %get-tuple-element.8.q_ref, ...), custom_call_target="tpu_custom_call" | custom-call | tf_op jit(solution)/shard_map/pallas_call | solution.py:188
  27.5 11.2 %all_to_all.9 = bf16[4,32,1792]{2,1,0:T(8,128)(2,1)S(1)} all-to-all(bf16[4,32,1792]{2,1,0:T(8,128)(2,1)} %bitcast.11), channel_id=1, replica_groups=mesh['req'=128,'tp'=4] {'tp'}, dimensions={0} | all-to-all | bytes 917504 | tf_op jit(solution)/shard_map/all_to_all | solution.py:204
  38.7 0.7 %fusion = bf16[32,1792]{1,0:T(8,128)(2,1)} fusion(bf16[4,32,1792]{2,1,0:T(8,128)(2,1)S(1)} %all_to_all.9), kind=kLoop, calls=%fused_computation.2 | loop fusion | flops 458752 | bytes 573440 | tf_op jit(solution)/shard_map/add | solution.py:208
Async XLA Ops:
  1.7 19.7 %collective-permute-start = (bf16[8,128,256]{2,1,0:T(8,128)(2,1)S(1)}, bf16[8,128,256]{2,1,0:T(8,128)(2,1)S(1)}, u32[]{:S(2)}, u32[]{:S(2)}) collective-permute-start(bf16[8,128,256]{2,1,0:T(8,128)(2,1)S(1)} %slice_bitcast_fusion), channel_id=1, source_target_pairs={{4,0},{8,4},{12,8},{16,12},{20,16},{24,20},{28,24},{32,28},{36,32}... | collective-permute-start | bytes 1572872 | tf_op jit(solution)/shard_map/ppermute | solution.py:169

commit v2 on v1

--- a/solution.py
+++ b/solution.py
@@ -196,8 +196,10 @@
             pltpu.SemaphoreType.DMA(()),
         ],
     )(
-        page_table, cache_len, packed, accum, stacked_q,
-        pltpu.with_memory_space_constraint(spill, pltpu.MemorySpace.VMEM), o_weight,
+        page_table, cache_len,
+        *[pltpu.with_memory_space_constraint(x, pltpu.MemorySpace.VMEM)
+          for x in (packed, accum, stacked_q, spill)],
+        o_weight,
     )
 
     parts = lax.axis_size("tp")

time: 39.7 us -> 43.7 us (1.10)
  local copies, waits for them, and re-layouts: 1.08 us -> 4.05 us
  Pallas kernels: 10.5 us -> 11.5 us
    unnamed x0 -> x6, local copies, waits for them, and re-layouts: none -> 2.97 us
    pallas_call x1, Pallas kernels: 6.04 us -> 7 us  [step(): pl.pallas_call(functools.partial(spill_kernel, own_slots), out_shape=jax....]
  transfers between devices with their start and end apart: 1 -> 1, of which waited for: 1 -> 1; matrix products, arithmetic and copies ran while one was open for 0% -> 0% of each run, Pallas kernels for 11% -> 10%
where the time goes in v2:
time: 43.7 us; the launch traced here: 43.3 us
  starting transfers between devices  13 us (30%)
  Pallas kernels  11.5 us (26%)
  blocking collectives  11.2 us (26%)
  local copies, waits for them, and re-layouts  4.05 us (9%)
  waiting for transfers between devices  2.16 us (5%)
  other arithmetic  0.7 us (2%)
  between operations  0.65 us (1%)
    ppermute x1, starting transfers between devices, step(): lax.ppermute(spill_source, 'req', [((i + 1) % ring, i) for i in range(rin...  13 us
    all_to_all x1, blocking collectives, step(): gathered = lax.all_to_all(partial, 'tp', 0, 0, tiled=True)  11.2 us
    pallas_call x1, Pallas kernels, step(): pl.pallas_call(functools.partial(spill_kernel, own_slots), out_shape=jax....  7 us
    pallas_call x1, Pallas kernels, step(): local_call(page_table, cache_len, accepted, parents, queries, tree_rows,...  4.51 us
    unnamed x6, local copies, waits for them, and re-layouts  2.97 us
    ppermute x1, waiting for transfers between devices, step(): lax.ppermute(spill_source, 'req', [((i + 1) % ring, i) for i in range(rin...  2.16 us
    slice x1, local copies, waits for them, and re-layouts, step(): spill_source = pool_slots[own_slots:]  1.08 us
  transfers between devices with their start and end apart: 1, of which 1 were waited for; matrix products, arithmetic and copies ran while one was open for 0% of the time, Pallas kernels for 10%

profile of v2, /device:TPU:8, one launch (start us, length us, event | category | flops | bytes accessed | tf_op | source)
XLA Modules:
  0.0 43.3 jit_solution(362065068854205896)
XLA Ops:
  0.6 1.1 %slice_bitcast_fusion = bf16[8,128,256]{2,1,0:T(8,128)(2,1)S(1)} fusion(bf16[12,1,128,256]{3,2,0,1:T(8,128)(2,1)} %bitcast.9), kind=kLoop, calls=%fused_computation | loop fusion | bytes 1048576 | tf_op jit(solution)/shard_map/slice | solution.py:168
  1.7 13.0 %collective-permute-start = (bf16[8,128,256]{2,1,0:T(8,128)(2,1)S(1)}, bf16[8,128,256]{2,1,0:T(8,128)(2,1)S(1)}, u32[]{:S(2)}, u32[]{:S(2)}) collective-permute-start(bf16[8,128,256]{2,1,0:T(8,128)(2,1)S(1)} %slice_bitcast_fusion), channel_id=1, source_target_pairs={{4,0},{8,4},{12,8},{16,12},{20,16},{24,20},{28,24},{32,28},{36,32}... | collective-permute-start | bytes 1572872 | tf_op jit(solution)/shard_map/ppermute | solution.py:169
  14.8 4.5 %shard_map.95 = (bf16[128,256]{1,0:T(8,128)(2,1)}, f32[2,448,128]{2,1,0:T(8,128)}, f32[2,448,128]{2,1,0:T(8,128)}, bf16[2,448,128]{2,1,0:T(8,128)(2,1)}) custom-call(s32[2,8]{1,0:T(2,128)} %table_ref.3, s32[2]{0:T(128)} %len_ref.3, s32[2]{0:T(128)} %leaf_ref.1, s32[2,64]{1,0:T(2,128)} %parents_ref.1, bf16[128,896]{1,0:T(8,128)(2,1)} %q_ref.1, ...), custom_call_target="tpu_custom_call" | custom-call | tf_op jit(solution)/shard_map/pallas_call | solution.py:185
  19.3 2.2 %collective-permute-done.spill_ref = bf16[8,128,256]{2,1,0:T(8,128)(2,1)S(1)} collective-permute-done((bf16[8,128,256]{2,1,0:T(8,128)(2,1)S(1)}, bf16[8,128,256]{2,1,0:T(8,128)(2,1)S(1)}, u32[]{:S(2)}, u32[]{:S(2)}) %collective-permute-start) | collective-permute-done | bytes 524320 | tf_op jit(solution)/shard_map/ppermute | solution.py:169
  21.4 0.0 copy-start
  21.4 1.0 %copy-done = f32[2,448,128]{2,1,0:T(8,128)S(1)} copy-done((f32[2,448,128]{2,1,0:T(8,128)S(1)}, f32[2,448,128]{2,1,0:T(8,128)}, u32[]{:S(2)}) %copy-start) | copy-done | bytes 458776
  22.5 0.0 copy-start.1
  22.5 1.0 %copy-done.1 = f32[2,448,128]{2,1,0:T(8,128)S(1)} copy-done((f32[2,448,128]{2,1,0:T(8,128)S(1)}, f32[2,448,128]{2,1,0:T(8,128)}, u32[]{:S(2)}) %copy-start.1) | copy-done | bytes 458776
  23.5 0.0 copy-start.2
  23.5 0.9 %copy-done.2 = bf16[2,448,128]{2,1,0:T(8,128)(2,1)S(1)} copy-done((bf16[2,448,128]{2,1,0:T(8,128)(2,1)S(1)}, bf16[2,448,128]{2,1,0:T(8,128)(2,1)}, u32[]{:S(2)}) %copy-start.2) | copy-done | bytes 229400
  24.4 7.0 %shard_map.96 = bf16[128,1792]{1,0:T(8,128)(2,1)} custom-call(s32[2,8]{1,0:T(2,128)} %table_ref.3, s32[2]{0:T(128)} %len_ref.3, f32[2,448,128]{2,1,0:T(8,128)S(1)} %copy-done, f32[2,448,128]{2,1,0:T(8,128)S(1)} %copy-done.1, bf16[2,448,128]{2,1,0:T(8,128)(2,1)S(1)} %copy-done.2, bf16[8,128,256]{2,1,0:T(8,128)(2,1)S(1)} %collective-permute-done.spill_ref, ...), custom_call_target="tpu_custom_call" | custom-call | tf_op jit(solution)/shard_map/pallas_call | solution.py:188
  31.4 11.2 %all_to_all.9 = bf16[4,32,1792]{2,1,0:T(8,128)(2,1)S(1)} all-to-all(bf16[4,32,1792]{2,1,0:T(8,128)(2,1)} %bitcast.11), channel_id=1, replica_groups=mesh['req'=128,'tp'=4] {'tp'}, dimensions={0} | all-to-all | bytes 917504 | tf_op jit(solution)/shard_map/all_to_all | solution.py:206
  42.6 0.7 %fusion = bf16[32,1792]{1,0:T(8,128)(2,1)} fusion(bf16[4,32,1792]{2,1,0:T(8,128)(2,1)S(1)} %all_to_all.9), kind=kLoop, calls=%fused_computation.2 | loop fusion | flops 458752 | bytes 573440 | tf_op jit(solution)/shard_map/add | solution.py:210
Async XLA Ops:
  1.7 19.7 %collective-permute-start = (bf16[8,128,256]{2,1,0:T(8,128)(2,1)S(1)}, bf16[8,128,256]{2,1,0:T(8,128)(2,1)S(1)}, u32[]{:S(2)}, u32[]{:S(2)}) collective-permute-start(bf16[8,128,256]{2,1,0:T(8,128)(2,1)S(1)} %slice_bitcast_fusion), channel_id=1, source_target_pairs={{4,0},{8,4},{12,8},{16,12},{20,16},{24,20},{28,24},{32,28},{36,32}... | collective-permute-start | bytes 1572872 | tf_op jit(solution)/shard_map/ppermute | solution.py:169
  21.4 1.0 %copy-start = (f32[2,448,128]{2,1,0:T(8,128)S(1)}, f32[2,448,128]{2,1,0:T(8,128)}, u32[]{:S(2)}) copy-start(f32[2,448,128]{2,1,0:T(8,128)} %get-tuple-element.6.ml_ref) | copy-start | bytes 1376260
  22.5 1.0 %copy-start.1 = (f32[2,448,128]{2,1,0:T(8,128)S(1)}, f32[2,448,128]{2,1,0:T(8,128)}, u32[]{:S(2)}) copy-start(f32[2,448,128]{2,1,0:T(8,128)} %get-tuple-element.7.a_ref) | copy-start | bytes 1376260
  23.5 0.9 %copy-start.2 = (bf16[2,448,128]{2,1,0:T(8,128)(2,1)S(1)}, bf16[2,448,128]{2,1,0:T(8,128)(2,1)}, u32[]{:S(2)}) copy-start(bf16[2,448,128]{2,1,0:T(8,128)(2,1)} %get-tuple-element.8.q_ref) | copy-start | bytes 688132
